TPU v7x, 32 devices: a whole 2x2x4 slice. The times are simulated.
32 devices in a mesh: grp: 8 (over y, x, core), rep: 4 (over z).
Axes of the slice: x: 2, y: 2, z: 4, core: 2. Of those that a mesh axis runs over, the one named last changes fastest.
Arguments:
- features: bfloat16 [4096, 256], P(('grp', 'rep')), may hold values from -0.0625 to 0.0625
- weight: bfloat16 [256, 256], replicated, may hold values from -0.375 to 0.375
- preact: bfloat16 [4096, 256], P(('grp', 'rep')), may hold values from -6 to 6
- grad_out: bfloat16 [4096, 256], P(('grp', 'rep')), may hold values from -1.5 to 1.5
- degree: int32 [4096], P(('grp', 'rep')), may hold values from 1 to 64
- tile_values: bfloat16 [256, 4, 128, 128], P(('grp', 'rep')), may hold values from 0 to 1
- tile_rows: int32 [256, 4], P(('grp', 'rep')), may hold values from -1 to 3, as said below
Outputs:
- input_grad: float32 [4096, 256], P(('grp', 'rep'))
- weight_grad: float32 [256, 256], replicated
Inputs may be any that keep to these rules, and one draw needn't show every extreme that they name: `tile_rows`: each of the 8 rows of one device (aligned blocks) has up to 4 live slots; in every such block some row has all 4 slots live.
All inputs are finite; a program needn't handle non-finite values.
Results may differ from a plain program's by a relative error of at most 0.013.
Values may be sent and summed in bfloat16 or wider, within the bound.
No kernel may reach another device: no remote copies, remote signals or barrier semaphores. Data moves between devices by JAX's collectives and lax.ppermute only.
A program may use at most 128 MiB of HBM per device.

v0:
```python
import jax
import jax.numpy as jnp
from jax import lax
from jax.sharding import PartitionSpec as P

HIGHEST = lax.Precision.HIGHEST


def gather_rep(x):
    reps = lax.axis_size("rep")
    me = lax.axis_index("rep")
    parts = [x]
    for shift in range(1, reps):
        parts.append(lax.ppermute(x, "rep", [((i + shift) % reps, i) for i in range(reps)]))
    stacked = jnp.stack(parts)
    return jnp.roll(stacked, me, axis=0)


def all_reduce_a2a(w, axes):
    count = 1
    for name in axes:
        count *= lax.axis_size(name)
    chunks = w.reshape(count, -1)
    owned = lax.all_to_all(chunks, axes, 0, 0, tiled=True).reshape(count, -1).sum(0)
    spread = jnp.broadcast_to(owned[None], (count, owned.shape[0]))
    return lax.all_to_all(spread, axes, 0, 0, tiled=True).reshape(w.shape)


def per_device(features, weight, preact, grad_out, degree, tile_values, tile_rows):
    rows_here, width = features.shape
    col_tiles, slots, edge, _ = tile_values.shape
    reps = lax.axis_size("rep")
    row_tiles = reps * rows_here // edge
    inverse = lax.rsqrt(degree.astype(jnp.float32))[:, None]
    grad_pre = jnp.where(preact > 0, grad_out, jnp.zeros_like(grad_out))
    scaled = (features.astype(jnp.float32) * inverse).astype(jnp.bfloat16)
    projected = (
        lax.dot_general(
            grad_pre, weight, (((1,), (1,)), ((), ())), preferred_element_type=jnp.float32
        )
        * inverse
    ).astype(jnp.bfloat16)
    columns = lax.all_gather(scaled, "grp", axis=0, tiled=True).reshape(col_tiles, edge, width)
    degree_lanes = jnp.broadcast_to(degree.astype(jnp.bfloat16)[:, None], (rows_here, 128))
    packed = jnp.concatenate([projected, grad_pre, degree_lanes], axis=1)
    block = gather_rep(packed).reshape(reps * rows_here, -1)
    block_proj = block[:, :width].reshape(row_tiles, edge, width)
    block_grad = block[:, width : 2 * width].astype(jnp.float32)
    block_inverse = lax.rsqrt(block[:, 2 * width : 2 * width + 1].astype(jnp.float32))
    tile_live = tile_rows >= 0
    clipped = jnp.where(tile_live, tile_rows, 0)
    onehot = (
        (clipped[..., None] == jnp.arange(row_tiles, dtype=jnp.int32)) & tile_live[..., None]
    ).astype(jnp.float32)
    product = jnp.einsum("csij,cjf->csif", tile_values, columns, preferred_element_type=jnp.float32)
    partial = jnp.einsum("csh,csif->hif", onehot, product, precision=HIGHEST)
    partial = partial.reshape(row_tiles * edge, width) * block_inverse
    weight_local = lax.dot_general(
        partial,
        block_grad,
        (((0,), (0,)), ((), ())),
        precision=HIGHEST,
        preferred_element_type=jnp.float32,
    )
    picked = jnp.take(block_proj, clipped, axis=0)
    picked = jnp.where(tile_live[:, :, None, None], picked, jnp.zeros_like(picked))
    result = jnp.einsum("csij,csif->cjf", tile_values, picked, preferred_element_type=jnp.float32)
    terms = lax.all_to_all(result, "grp", 0, 0, tiled=True)
    input_grad = terms.sum(0) * inverse
    weight_grad = all_reduce_a2a(weight_local, ("grp", "rep"))
    return (input_grad, weight_grad)


def solution(mesh):
    return jax.shard_map(
        per_device,
        mesh=mesh,
        in_specs=(
            P(("grp", "rep"), None),
            P(),
            P(("grp", "rep"), None),
            P(("grp", "rep"), None),
            P(("grp", "rep")),
            P(("grp", "rep"), None, None, None),
            P(("grp", "rep"), None),
        ),
        out_specs=(P(("grp", "rep"), None), P()),
        check_vma=False,
    )
```

profile of v0, /device:TPU:0, one launch (start us, length us, event | category | flops | bytes accessed | tf_op | source)
XLA Modules:
  0.0 101.6 jit_solution(6074562311005059718)
XLA Ops:
  0.6 0.7 convert_rsqrt_fusion
  1.4 0.7 convert_element_type.22
  2.1 0.9 compare_select_fusion
  2.9 1.1 %fusion.8 = bf16[128,256]{1,0:T(8,128)(2,1)S(1)} fusion(bf16[128,256]{1,0:T(8,128)(2,1)S(1)} %compare_select_fusion, bf16[256,256]{1,0:T(8,128)(2,1)} %param.8, f32[128]{0:T(128)S(1)} %convert_rsqrt_fusion), kind=kOutput, calls=%fused_computation.10 | convolution fusion | flops 16842752 | bytes 262656 | tf_op jit(solution)/shard_map/dot_general | solution.py:38
  4.2 5.1 %collective-permute-start = (bf16[128,640]{1,0:T(8,128)(2,1)S(1)}, bf16[128,640]{1,0:T(8,128)(2,1)S(1)}, u32[]{:S(2)}, u32[]{:S(2)}) collective-permute-start(bf16[128,640]{1,0:T(8,128)(2,1)S(1)} %pad_maximum_fusion), channel_id=1, source_target_pairs={{1,0},{2,1},{3,2},{0,3},{5,4},{6,5},{7,6},{4,7},{9,8},{10,9},{11,1... | collective-permute-start | bytes 491528 | tf_op jit(solution)/shard_map/ppermute | solution.py:14
  9.3 1.0 collective-permute-start.2
  10.3 0.7 broadcast_select_fusion
  11.0 0.7 broadcast_compare_fusion
  12.1 1.9 %collective-permute-done = bf16[128,640]{1,0:T(8,128)(2,1)S(1)} collective-permute-done((bf16[128,640]{1,0:T(8,128)(2,1)S(1)}, bf16[128,640]{1,0:T(8,128)(2,1)S(1)}, u32[]{:S(2)}, u32[]{:S(2)}) %collective-permute-start) | collective-permute-done | bytes 163872 | tf_op jit(solution)/shard_map/ppermute | solution.py:14
  13.9 9.2 %collective-permute-done.1 = bf16[128,640]{1,0:T(8,128)(2,1)S(1)} collective-permute-done((bf16[128,640]{1,0:T(8,128)(2,1)S(1)}, bf16[128,640]{1,0:T(8,128)(2,1)S(1)}, u32[]{:S(2)}, u32[]{:S(2)}) %collective-permute-start.1) | collective-permute-done | bytes 163872 | tf_op jit(solution)/shard_map/ppermute | solution.py:14
  23.4 0.8 copy-done.1
  24.3 0.7 gather_fusion
  24.9 2.4 %copy.28 = bf16[8,4,128,256]{2,3,1,0:T(8,128)(2,1)} copy(bf16[8,4,128,256]{3,2,1,0:T(8,128)(2,1)S(1)} %bitcast.43) | data formatting | bytes 4194304 | tf_op jit(solution)/shard_map/jit(_take)/gather | solution.py:65
  27.3 3.3 %fusion.5 = f32[8,128,256]{1,2,0:T(8,128)} fusion(bf16[8,4,128,128]{3,2,1,0:T(8,128)(2,1)S(1)} %copy-done, bf16[8,4,128,256]{2,3,1,0:T(8,128)(2,1)} %copy.28, pred[8,4]{1,0:T(8,128)(4,1)S(1)} %copy.26, pred[8,4]{1,0:T(8,128)(4,1)S(1)} %copy.25), kind=kOutput, calls=%fused_computation.7 | convolution fusion | flops 270532608 | bytes 4194368 | tf_op jit(solution)/shard_map/csij,csif->cjf/dot_general | solution.py:67
  30.7 3.9 %all-to-all-start = ((f32[8,128,256]{1,2,0:T(8,128)}), f32[8,128,256]{1,2,0:T(8,128)S(1)}, u32[]{:S(2)}, u32[]{:S(2)}) async-start(f32[8,128,256]{1,2,0:T(8,128)} %fusion.5), calls=%async_computation | async-start | bytes 2097152 | tf_op jit(solution)/shard_map/all_to_all | solution.py:68
  34.7 15.2 %all-to-all-done = f32[8,128,256]{1,2,0:T(8,128)S(1)} async-done(((f32[8,128,256]{1,2,0:T(8,128)}), f32[8,128,256]{1,2,0:T(8,128)S(1)}, u32[]{:S(2)}, u32[]{:S(2)}) %all-to-all-start) | async-done | bytes 1048608 | tf_op jit(solution)/shard_map/all_to_all | solution.py:68
  50.1 0.7 multiply_convert_fusion
  50.9 8.9 %all_gather.3 = bf16[1024,256]{1,0:T(8,128)(2,1)S(1)} all-gather(bf16[128,256]{1,0:T(8,128)(2,1)S(1)} %get-tuple-element.6), channel_id=1, replica_groups=mesh['grp'=8,'rep'=4] {'grp'}, dimensions={0}, use_global_device_ids=true | all-gather | bytes 589824 | tf_op jit(solution)/shard_map/all_gather | solution.py:43
  59.8 2.7 %convolution_bitcast_fusion = f32[8,4,128,256]{2,3,1,0:T(8,128)} fusion(bf16[8,128,256,1]{2,1,3,0:T(8,128)(2,1)S(1)} %bitcast.47, bf16[8,4,128,128]{3,2,1,0:T(8,128)(2,1)S(1)} %copy-done), kind=kOutput, calls=%fused_computation.1 | convolution fusion | flops 268435456 | bytes 5767168 | tf_op jit(solution)/shard_map/csij,cjf->csif/dot_general | solution.py:55
  62.5 5.5 %copy.31 = f32[8,4,128,256]{3,0,1,2:T(8,128)} copy(f32[8,4,128,256]{2,3,1,0:T(8,128)} %convolution_bitcast_fusion) | data formatting | bytes 8388608 | tf_op jit(solution)/shard_map/csij,cjf->csif/dot_general | solution.py:55
  68.0 4.0 %convolution_bitcast_fusion.1 = f32[4,128,256]{2,0,1:T(4,128)S(1)} fusion(f32[8,4,128,256]{3,0,1,2:T(8,128)} %copy.31, s32[8,4]{0,1:T(4,128)S(1)} %get-tuple-element.2, pred[8,4]{0,1:T(4,128)(4,1)S(1)} %get-tuple-element.4), kind=kOutput, calls=%fused_computation.8 | convolution fusion | flops 50331904 | bytes 4718752 | tf_op jit(solution)/shard_map/csh,csif->hif/dot_general | solution.py:56
  73.1 14.0 %all_to_all.21 = f32[32,1,2048]{2,1,0:T(1,128)S(1)} all-to-all(f32[32,1,2048]{2,1,0:T(1,128)S(1)} %all_to_all.17), channel_id=1, replica_groups=mesh['grp'=8,'rep'=4] {'grp','rep'}, dimensions={0} | all-to-all | bytes 524288 | tf_op jit(solution)/shard_map/all_to_all | solution.py:24
  87.5 12.7 %all_to_all.22 = f32[32,1,2048]{2,1,0:T(1,128)S(1)} all-to-all(f32[32,1,2048]{2,1,0:T(1,128)S(1)} %broadcast_in_dim.48), channel_id=1, replica_groups=mesh['grp'=8,'rep'=4] {'grp','rep'}, dimensions={0} | all-to-all | bytes 524288 | tf_op jit(solution)/shard_map/all_to_all | solution.py:26
  100.8 0.7 reshape.44
  (36 shorter events, 3.1 us)
Async XLA Ops:
  0.6 26.7 %copy-start = (bf16[8,4,128,128]{3,2,1,0:T(8,128)(2,1)S(1)}, bf16[8,4,128,128]{3,2,1,0:T(8,128)(2,1)}, u32[]{:S(2)}) copy-start(bf16[8,4,128,128]{3,2,1,0:T(8,128)(2,1)} %param.12) | copy-start | bytes 3145732
  4.2 9.8 %collective-permute-start = (bf16[128,640]{1,0:T(8,128)(2,1)S(1)}, bf16[128,640]{1,0:T(8,128)(2,1)S(1)}, u32[]{:S(2)}, u32[]{:S(2)}) collective-permute-start(bf16[128,640]{1,0:T(8,128)(2,1)S(1)} %pad_maximum_fusion), channel_id=1, source_target_pairs={{1,0},{2,1},{3,2},{0,3},{5,4},{6,5},{7,6},{4,7},{9,8},{10,9},{11,1... | collective-permute-start | bytes 491528 | tf_op jit(solution)/shard_map/ppermute | solution.py:14
  9.3 13.9 %collective-permute-start.1 = (bf16[128,640]{1,0:T(8,128)(2,1)S(1)}, bf16[128,640]{1,0:T(8,128)(2,1)S(1)}, u32[]{:S(2)}, u32[]{:S(2)}) collective-permute-start(bf16[128,640]{1,0:T(8,128)(2,1)S(1)} %pad_maximum_fusion), channel_id=1, source_target_pairs={{2,0},{3,1},{0,2},{1,3},{6,4},{7,5},{4,6},{5,7},{10,8},{11,9},{8,1... | collective-permute-start | bytes 491528 | tf_op jit(solution)/shard_map/ppermute | solution.py:14
  9.3 13.9 %collective-permute-start.2 = (bf16[128,640]{1,0:T(8,128)(2,1)S(1)}, bf16[128,640]{1,0:T(8,128)(2,1)S(1)}, u32[]{:S(2)}, u32[]{:S(2)}) collective-permute-start(bf16[128,640]{1,0:T(8,128)(2,1)S(1)} %pad_maximum_fusion), channel_id=1, source_target_pairs={{3,0},{0,1},{1,2},{2,3},{7,4},{4,5},{5,6},{6,7},{11,8},{8,9},{9,10... | collective-permute-start | bytes 491528 | tf_op jit(solution)/shard_map/ppermute | solution.py:14
  23.4 0.8 copy-start.1
  30.7 3.9 %copy-start.2 = (bf16[4,128,640]{2,1,0:T(8,128)(2,1)S(1)}, bf16[4,128,640]{2,1,0:T(8,128)(2,1)}, u32[]{:S(2)}) copy-start(bf16[4,128,640]{2,1,0:T(8,128)(2,1)} %copy-done.1) | copy-start | bytes 1966084
  30.7 19.3 %all-to-all-start = ((f32[8,128,256]{1,2,0:T(8,128)}), f32[8,128,256]{1,2,0:T(8,128)S(1)}, u32[]{:S(2)}, u32[]{:S(2)}) async-start(f32[8,128,256]{1,2,0:T(8,128)} %fusion.5), calls=%async_computation | async-start | bytes 2097152 | tf_op jit(solution)/shard_map/all_to_all | solution.py:68
  34.6 15.6 %copy-start.3 = (bf16[128,256]{1,0:T(8,128)(2,1)S(1)}, bf16[128,256]{1,0:T(8,128)(2,1)}, u32[]{:S(2)}) copy-start(bf16[128,256]{1,0:T(8,128)(2,1)} %param.7) | copy-start | bytes 196612
where the time goes:
time: 102 us
  blocking collectives  35.7 us (35%)
  waiting for transfers between devices  26.3 us (26%)
  matrix products  11.8 us (12%)
  local copies, waits for them, and re-layouts  11.4 us (11%)
  starting transfers between devices  9.98 us (10%)
  other arithmetic  5.58 us (5%)
    all_to_all x1, waiting for transfers between devices, per_device(): terms = lax.all_to_all(result, 'grp', 0, 0, tiled=True)  15.2 us
    all_to_all x1, blocking collectives, all_reduce_a2a(): lax.all_to_all(chunks, axes, 0, 0, tiled=True).reshape(count, -1).sum(0)  14 us
    all_to_all x1, blocking collectives, all_reduce_a2a(): return lax.all_to_all(spread, axes, 0, 0, tiled=True).reshape(w.shape)  12.7 us
    ppermute x3, waiting for transfers between devices, gather_rep(): lax.ppermute(x, 'rep', [((i + shift) % reps, i) for i in range(reps)])  11.1 us
    all_gather x1, blocking collectives, per_device(): lax.all_gather(scaled, 'grp', axis=0, tiled=True)  8.89 us
    ppermute x3, starting transfers between devices, gather_rep(): lax.ppermute(x, 'rep', [((i + shift) % reps, i) for i in range(reps)])  6.12 us
    dot_general x1, local copies, waits for them, and re-layouts, per_device(): jnp.einsum('csij,cjf->csif', tile_values, columns, preferred_element_type...  5.51 us
    dot_general x1, matrix products, per_device(): partial = jnp.einsum('csh,csif->hif', onehot, product, precision=HIGHEST)  4.02 us
  transfers between devices with their start and end apart: 4, of which 3 were waited for; matrix products, arithmetic and copies ran while one was open for 2% of the time, Pallas kernels for 0%

commit v1 on v0

--- a/solution.py
+++ b/solution.py
@@ -4,6 +4,18 @@
 from jax.sharding import PartitionSpec as P
 
 HIGHEST = lax.Precision.HIGHEST
+
+
+def doubled_up(shard, axis, dim):
+    ways, here, step = (lax.axis_size(axis), lax.axis_index(axis), shard.shape[dim])
+    line, have = (shard, 1)
+    while have < ways:
+        line = jnp.concatenate(
+            [line, lax.ppermute(line, axis, [(d, (d - have) % ways) for d in range(ways)])],
+            axis=dim,
+        )
+        have = 2 * have
+    return jnp.roll(line, here * step, axis=dim)
 
 
 def gather_rep(x):
@@ -40,7 +52,7 @@
         )
         * inverse
     ).astype(jnp.bfloat16)
-    columns = lax.all_gather(scaled, "grp", axis=0, tiled=True).reshape(col_tiles, edge, width)
+    columns = doubled_up(scaled, "grp", 0).reshape(col_tiles, edge, width)
     degree_lanes = jnp.broadcast_to(degree.astype(jnp.bfloat16)[:, None], (rows_here, 128))
     packed = jnp.concatenate([projected, grad_pre, degree_lanes], axis=1)
     block = gather_rep(packed).reshape(reps * rows_here, -1)

time: 102 us -> 95 us (0.931)
  blocking collectives: 35.7 us -> 0 us
  waiting for transfers between devices: 26.3 us -> 40.9 us
  starting transfers between devices: 9.98 us -> 21.2 us
  other arithmetic: 5.58 us -> 7.48 us
    all_to_all x2 -> x0, blocking collectives: 26.8 us -> none  [the longest x1 14 us: all_reduce_a2a(): lax.all_to_all(chunks, axes, 0, 0, tiled=True).reshape(count, -1).sum(0)]
    all_to_all x0 -> x2, waiting for transfers between devices: none -> 12.7 us  [the longest x1 9.29 us: all_reduce_a2a(): return lax.all_to_all(spread, axes, 0, 0, tiled=True).reshape(w.shape)]
    all_gather x1 -> x0, blocking collectives: 8.89 us -> none  [per_device(): lax.all_gather(scaled, 'grp', axis=0, tiled=True)]
    all_to_all x0 -> x2, starting transfers between devices: none -> 7.38 us  [the longest x1 4.8 us: all_reduce_a2a(): lax.all_to_all(chunks, axes, 0, 0, tiled=True).reshape(count, -1).sum(0)]
    ppermute x0 -> x3, waiting for transfers between devices: none -> 6.54 us  [doubled_up(): lax.ppermute(line, axis, [(d, (d - have) % ways) for d in range(ways)])]
    ppermute x0 -> x3, starting transfers between devices: none -> 4.14 us  [doubled_up(): lax.ppermute(line, axis, [(d, (d - have) % ways) for d in range(ways)])]
    ppermute x3, waiting for transfers between devices: 11.1 us -> 7.43 us  [gather_rep(): lax.ppermute(x, 'rep', [((i + shift) % reps, i) for i in range(reps)])]
  transfers between devices with their start and end apart: 4 -> 9, of which waited for: 3 -> 6; matrix products, arithmetic and copies ran while one was open for 2% -> 12% of each run, Pallas kernels for 0% -> 0%
where the time goes in v1:
time: 95 us; the launch traced here: 94.3 us
  waiting for transfers between devices  40.9 us (43%)
  starting transfers between devices  21.2 us (22%)
  local copies, waits for them, and re-layouts  12.1 us (13%)
  matrix products  11.8 us (12%)
  other arithmetic  7.48 us (8%)
    all_to_all x1, waiting for transfers between devices, per_device(): terms = lax.all_to_all(result, 'grp', 0, 0, tiled=True)  14.2 us
    all_to_all x1, waiting for transfers between devices, all_reduce_a2a(): return lax.all_to_all(spread, axes, 0, 0, tiled=True).reshape(w.shape)  9.29 us
    ppermute x3, waiting for transfers between devices, gather_rep(): lax.ppermute(x, 'rep', [((i + shift) % reps, i) for i in range(reps)])  7.43 us
    ppermute x3, waiting for transfers between devices, doubled_up(): lax.ppermute(line, axis, [(d, (d - have) % ways) for d in range(ways)])  6.54 us
    ppermute x3, starting transfers between devices, gather_rep(): lax.ppermute(x, 'rep', [((i + shift) % reps, i) for i in range(reps)])  6.12 us
    dot_general x1, local copies, waits for them, and re-layouts, per_device(): jnp.einsum('csij,cjf->csif', tile_values, columns, preferred_element_type...  5.5 us
    all_to_all x1, starting transfers between devices, all_reduce_a2a(): lax.all_to_all(chunks, axes, 0, 0, tiled=True).reshape(count, -1).sum(0)  4.8 us
    ppermute x3, starting transfers between devices, doubled_up(): lax.ppermute(line, axis, [(d, (d - have) % ways) for d in range(ways)])  4.14 us
  transfers between devices with their start and end apart: 9, of which 6 were waited for; matrix products, arithmetic and copies ran while one was open for 12% of the time, Pallas kernels for 0%

profile of v1, /device:TPU:0, one launch (start us, length us, event | category | flops | bytes accessed | tf_op | source)
XLA Modules:
  0.0 94.3 jit_solution(4907564032630039334)
XLA Ops:
  2.1 0.9 compare_select_fusion
  2.9 1.1 %fusion.8 = bf16[128,256]{1,0:T(8,128)(2,1)S(1)} fusion(bf16[128,256]{1,0:T(8,128)(2,1)S(1)} %compare_select_fusion, bf16[256,256]{1,0:T(8,128)(2,1)} %param.8, f32[128]{0:T(128)S(1)} %convert_rsqrt_fusion), kind=kOutput, calls=%fused_computation.10 | convolution fusion | flops 16842752 | bytes 262656 | tf_op jit(solution)/shard_map/dot_general | solution.py:50
  4.2 5.1 %collective-permute-start = (bf16[128,640]{1,0:T(8,128)(2,1)S(1)}, bf16[128,640]{1,0:T(8,128)(2,1)S(1)}, u32[]{:S(2)}, u32[]{:S(2)}) collective-permute-start(bf16[128,640]{1,0:T(8,128)(2,1)S(1)} %pad_maximum_fusion.1), channel_id=1, source_target_pairs={{1,0},{2,1},{3,2},{0,3},{5,4},{6,5},{7,6},{4,7},{9,8},{10,9},{11,1... | collective-permute-start | bytes 491528 | tf_op jit(solution)/shard_map/ppermute | solution.py:26
  9.3 1.0 %collective-permute-start.2 = (bf16[128,640]{1,0:T(8,128)(2,1)S(1)}, bf16[128,640]{1,0:T(8,128)(2,1)S(1)}, u32[]{:S(2)}, u32[]{:S(2)}) collective-permute-start(bf16[128,640]{1,0:T(8,128)(2,1)S(1)} %pad_maximum_fusion.1), channel_id=1, source_target_pairs={{3,0},{0,1},{1,2},{2,3},{7,4},{4,5},{5,6},{6,7},{11,8},{8,9},{9,10... | collective-permute-start | bytes 491528 | tf_op jit(solution)/shard_map/ppermute | solution.py:26
  10.3 0.9 constant_dynamic-update-slice_fusion.7
  11.2 1.1 %collective-permute-start.3 = (bf16[128,256]{1,0:T(8,128)(2,1)S(1)}, bf16[128,256]{1,0:T(8,128)(2,1)S(1)}, u32[]{:S(2)}, u32[]{:S(2)}) collective-permute-start(bf16[128,256]{1,0:T(8,128)(2,1)S(1)} %get-tuple-element.3), channel_id=1, source_target_pairs={{0,28},{4,0},{8,4},{12,8},{16,12},{20,16},{24,20},{28,24},{1,29},{... | collective-permute-start | bytes 196616 | tf_op jit(solution)/shard_map/ppermute | solution.py:14
  14.2 1.5 %collective-permute-start.4 = (bf16[256,256]{1,0:T(8,128)(2,1)S(1)}, bf16[256,256]{1,0:T(8,128)(2,1)S(1)}, u32[]{:S(2)}, u32[]{:S(2)}) collective-permute-start(bf16[256,256]{1,0:T(8,128)(2,1)S(1)} %pad_maximum_fusion.2), channel_id=1, source_target_pairs={{0,24},{4,28},{8,0},{12,4},{16,8},{20,12},{24,16},{28,20},{1,25},{... | collective-permute-start | bytes 393224 | tf_op jit(solution)/shard_map/ppermute | solution.py:14
  15.7 7.4 %collective-permute-done.1 = bf16[128,640]{1,0:T(8,128)(2,1)S(1)} collective-permute-done((bf16[128,640]{1,0:T(8,128)(2,1)S(1)}, bf16[128,640]{1,0:T(8,128)(2,1)S(1)}, u32[]{:S(2)}, u32[]{:S(2)}) %collective-permute-start.1) | collective-permute-done | bytes 163872 | tf_op jit(solution)/shard_map/ppermute | solution.py:26
  23.4 1.6 %collective-permute-start.5 = (bf16[512,256]{1,0:T(8,128)(2,1)S(1)}, bf16[512,256]{1,0:T(8,128)(2,1)S(1)}, u32[]{:S(2)}, u32[]{:S(2)}) collective-permute-start(bf16[512,256]{1,0:T(8,128)(2,1)S(1)} %pad_maximum_fusion), channel_id=1, source_target_pairs={{0,16},{4,20},{8,24},{12,28},{16,0},{20,4},{24,8},{28,12},{1,17},{... | collective-permute-start | bytes 786440 | tf_op jit(solution)/shard_map/ppermute | solution.py:14
  25.2 6.0 %collective-permute-done.5 = bf16[512,256]{1,0:T(8,128)(2,1)S(1)} collective-permute-done((bf16[512,256]{1,0:T(8,128)(2,1)S(1)}, bf16[512,256]{1,0:T(8,128)(2,1)S(1)}, u32[]{:S(2)}, u32[]{:S(2)}) %collective-permute-start.5) | collective-permute-done | bytes 262176 | tf_op jit(solution)/shard_map/ppermute | solution.py:14
  31.4 2.7 %convolution_bitcast_fusion = f32[8,4,128,256]{2,3,1,0:T(8,128)} fusion(bf16[8,128,256,1]{2,1,3,0:T(8,128)(2,1)S(1)} %bitcast.47, bf16[8,4,128,128]{3,2,1,0:T(8,128)(2,1)S(1)} %copy-done), kind=kOutput, calls=%fused_computation.1 | convolution fusion | flops 268435456 | bytes 5767168 | tf_op jit(solution)/shard_map/csij,cjf->csif/dot_general | solution.py:67
  34.1 5.5 %copy.37 = f32[8,4,128,256]{3,0,1,2:T(8,128)} copy(f32[8,4,128,256]{2,3,1,0:T(8,128)} %convolution_bitcast_fusion) | data formatting | bytes 8388608 | tf_op jit(solution)/shard_map/csij,cjf->csif/dot_general | solution.py:67
  39.6 4.0 %convolution_bitcast_fusion.1 = f32[4,128,256]{2,0,1:T(4,128)S(1)} fusion(f32[8,4,128,256]{3,0,1,2:T(8,128)} %copy.37, s32[8,4]{0,1:T(4,128)S(1)} %get-tuple-element.4, pred[8,4]{0,1:T(4,128)(4,1)S(1)} %get-tuple-element.6), kind=kOutput, calls=%fused_computation.8 | convolution fusion | flops 50331904 | bytes 4718752 | tf_op jit(solution)/shard_map/csh,csif->hif/dot_general | solution.py:68
  44.5 1.0 %all_to_all.17 = f32[32,1,2048]{2,1,0:T(1,128)} reshape(f32[256,256]{1,0:T(8,128)S(1)} %fusion.11) | data formatting | bytes 524288 | tf_op jit(solution)/shard_map/all_to_all | solution.py:36
  45.4 4.8 %all-to-all-start.1 = ((f32[32,1,2048]{2,1,0:T(1,128)}), f32[32,1,2048]{2,1,0:T(1,128)}, u32[]{:S(2)}, u32[]{:S(2)}) async-start(f32[32,1,2048]{2,1,0:T(1,128)} %all_to_all.17), calls=%async_computation.1 | async-start | bytes 524288 | tf_op jit(solution)/shard_map/all_to_all | solution.py:36
  51.3 2.4 %copy.34 = bf16[8,4,128,256]{2,3,1,0:T(8,128)(2,1)} copy(bf16[8,4,128,256]{3,2,1,0:T(8,128)(2,1)S(1)} %bitcast.43) | data formatting | bytes 4194304 | tf_op jit(solution)/shard_map/jit(_take)/gather | solution.py:77
  53.7 3.3 %fusion.5 = f32[8,128,256]{1,2,0:T(8,128)} fusion(bf16[8,4,128,128]{3,2,1,0:T(8,128)(2,1)S(1)} %copy-done, bf16[8,4,128,256]{2,3,1,0:T(8,128)(2,1)} %copy.34, pred[8,4]{1,0:T(8,128)(4,1)S(1)} %copy.32, pred[8,4]{1,0:T(8,128)(4,1)S(1)} %copy.31), kind=kOutput, calls=%fused_computation.7 | convolution fusion | flops 270532608 | bytes 4194368 | tf_op jit(solution)/shard_map/csij,csif->cjf/dot_general | solution.py:79
  57.0 3.4 %all-to-all-done.1 = f32[32,1,2048]{2,1,0:T(1,128)} async-done(((f32[32,1,2048]{2,1,0:T(1,128)}), f32[32,1,2048]{2,1,0:T(1,128)}, u32[]{:S(2)}, u32[]{:S(2)}) %all-to-all-start.1) | async-done | bytes 262176 | tf_op jit(solution)/shard_map/all_to_all | solution.py:36
  60.4 3.6 %all-to-all-start = ((f32[8,128,256]{1,2,0:T(8,128)}), f32[8,128,256]{1,2,0:T(8,128)S(1)}, u32[]{:S(2)}, u32[]{:S(2)}) async-start(f32[8,128,256]{1,2,0:T(8,128)} %fusion.5), calls=%async_computation | async-start | bytes 2097152 | tf_op jit(solution)/shard_map/all_to_all | solution.py:80
  64.0 1.1 %reduce_sum.19 = f32[2048]{0:T(1024)S(1)} reduce(f32[32,1,2048]{2,1,0:T(1,128)} %all-to-all-done.1, f32[]{:T(128)} %constant.65.clone.1), dimensions={0,1}, to_apply=%region_1.2 | reduce | flops 63488 | bytes 270340 | tf_op jit(solution)/shard_map/reduce_sum | solution.py:36
  65.1 14.2 %all-to-all-done = f32[8,128,256]{1,2,0:T(8,128)S(1)} async-done(((f32[8,128,256]{1,2,0:T(8,128)}), f32[8,128,256]{1,2,0:T(8,128)S(1)}, u32[]{:S(2)}, u32[]{:S(2)}) %all-to-all-start) | async-done | bytes 1048608 | tf_op jit(solution)/shard_map/all_to_all | solution.py:80
  79.3 0.8 broadcast_in_dim.48
  80.2 2.6 %all-to-all-start.2 = ((f32[32,1,2048]{2,1,0:T(1,128)}), f32[32,1,2048]{2,1,0:T(1,128)S(1)}, u32[]{:S(2)}, u32[]{:S(2)}) async-start(f32[32,1,2048]{2,1,0:T(1,128)} %broadcast_in_dim.48), calls=%async_computation.2 | async-start | bytes 524288 | tf_op jit(solution)/shard_map/all_to_all | solution.py:38
  83.7 9.3 %all-to-all-done.2 = f32[32,1,2048]{2,1,0:T(1,128)S(1)} async-done(((f32[32,1,2048]{2,1,0:T(1,128)}), f32[32,1,2048]{2,1,0:T(1,128)S(1)}, u32[]{:S(2)}, u32[]{:S(2)}) %all-to-all-start.2) | async-done | bytes 262176 | tf_op jit(solution)/shard_map/all_to_all | solution.py:38
  (48 shorter events, 8.1 us)
Async XLA Ops:
  0.6 30.7 %copy-start = (bf16[8,4,128,128]{3,2,1,0:T(8,128)(2,1)S(1)}, bf16[8,4,128,128]{3,2,1,0:T(8,128)(2,1)}, u32[]{:S(2)}) copy-start(bf16[8,4,128,128]{3,2,1,0:T(8,128)(2,1)} %param.12) | copy-start | bytes 3145732
  4.2 11.5 %collective-permute-start = (bf16[128,640]{1,0:T(8,128)(2,1)S(1)}, bf16[128,640]{1,0:T(8,128)(2,1)S(1)}, u32[]{:S(2)}, u32[]{:S(2)}) collective-permute-start(bf16[128,640]{1,0:T(8,128)(2,1)S(1)} %pad_maximum_fusion.1), channel_id=1, source_target_pairs={{1,0},{2,1},{3,2},{0,3},{5,4},{6,5},{7,6},{4,7},{9,8},{10,9},{11,1... | collective-permute-start | bytes 491528 | tf_op jit(solution)/shard_map/ppermute | solution.py:26
  9.3 13.9 %collective-permute-start.1 = (bf16[128,640]{1,0:T(8,128)(2,1)S(1)}, bf16[128,640]{1,0:T(8,128)(2,1)S(1)}, u32[]{:S(2)}, u32[]{:S(2)}) collective-permute-start(bf16[128,640]{1,0:T(8,128)(2,1)S(1)} %pad_maximum_fusion.1), channel_id=1, source_target_pairs={{2,0},{3,1},{0,2},{1,3},{6,4},{7,5},{4,6},{5,7},{10,8},{11,9},{8,1... | collective-permute-start | bytes 491528 | tf_op jit(solution)/shard_map/ppermute | solution.py:26
  9.3 13.9 %collective-permute-start.2 = (bf16[128,640]{1,0:T(8,128)(2,1)S(1)}, bf16[128,640]{1,0:T(8,128)(2,1)S(1)}, u32[]{:S(2)}, u32[]{:S(2)}) collective-permute-start(bf16[128,640]{1,0:T(8,128)(2,1)S(1)} %pad_maximum_fusion.1), channel_id=1, source_target_pairs={{3,0},{0,1},{1,2},{2,3},{7,4},{4,5},{5,6},{6,7},{11,8},{8,9},{9,10... | collective-permute-start | bytes 491528 | tf_op jit(solution)/shard_map/ppermute | solution.py:26
  11.2 3.0 %collective-permute-start.3 = (bf16[128,256]{1,0:T(8,128)(2,1)S(1)}, bf16[128,256]{1,0:T(8,128)(2,1)S(1)}, u32[]{:S(2)}, u32[]{:S(2)}) collective-permute-start(bf16[128,256]{1,0:T(8,128)(2,1)S(1)} %get-tuple-element.3), channel_id=1, source_target_pairs={{0,28},{4,0},{8,4},{12,8},{16,12},{20,16},{24,20},{28,24},{1,29},{... | collective-permute-start | bytes 196616 | tf_op jit(solution)/shard_map/ppermute | solution.py:14
  14.2 9.1 %collective-permute-start.4 = (bf16[256,256]{1,0:T(8,128)(2,1)S(1)}, bf16[256,256]{1,0:T(8,128)(2,1)S(1)}, u32[]{:S(2)}, u32[]{:S(2)}) collective-permute-start(bf16[256,256]{1,0:T(8,128)(2,1)S(1)} %pad_maximum_fusion.2), channel_id=1, source_target_pairs={{0,24},{4,28},{8,0},{12,4},{16,8},{20,12},{24,16},{28,20},{1,25},{... | collective-permute-start | bytes 393224 | tf_op jit(solution)/shard_map/ppermute | solution.py:14
  23.4 7.8 %collective-permute-start.5 = (bf16[512,256]{1,0:T(8,128)(2,1)S(1)}, bf16[512,256]{1,0:T(8,128)(2,1)S(1)}, u32[]{:S(2)}, u32[]{:S(2)}) collective-permute-start(bf16[512,256]{1,0:T(8,128)(2,1)S(1)} %pad_maximum_fusion), channel_id=1, source_target_pairs={{0,16},{4,20},{8,24},{12,28},{16,0},{20,4},{24,8},{28,12},{1,17},{... | collective-permute-start | bytes 786440 | tf_op jit(solution)/shard_map/ppermute | solution.py:14
  45.4 15.0 %all-to-all-start.1 = ((f32[32,1,2048]{2,1,0:T(1,128)}), f32[32,1,2048]{2,1,0:T(1,128)}, u32[]{:S(2)}, u32[]{:S(2)}) async-start(f32[32,1,2048]{2,1,0:T(1,128)} %all_to_all.17), calls=%async_computation.1 | async-start | bytes 524288 | tf_op jit(solution)/shard_map/all_to_all | solution.py:36
  60.4 18.9 %all-to-all-start = ((f32[8,128,256]{1,2,0:T(8,128)}), f32[8,128,256]{1,2,0:T(8,128)S(1)}, u32[]{:S(2)}, u32[]{:S(2)}) async-start(f32[8,128,256]{1,2,0:T(8,128)} %fusion.5), calls=%async_computation | async-start | bytes 2097152 | tf_op jit(solution)/shard_map/all_to_all | solution.py:80
  80.2 12.8 %all-to-all-start.2 = ((f32[32,1,2048]{2,1,0:T(1,128)}), f32[32,1,2048]{2,1,0:T(1,128)S(1)}, u32[]{:S(2)}, u32[]{:S(2)}) async-start(f32[32,1,2048]{2,1,0:T(1,128)} %broadcast_in_dim.48), calls=%async_computation.2 | async-start | bytes 524288 | tf_op jit(solution)/shard_map/all_to_all | solution.py:38
